TPU v7x, 512 devices: a whole 4x4x16 slice. The times are simulated.
512 devices in a mesh: path: 32 (over x, y, core), tensor: 16 (over z).
Axes of the slice: x: 4, y: 4, z: 16, core: 2. Of those that a mesh axis runs over, the one named last changes fastest.
Arguments:
- hidden_in: bfloat16 [12288, 2048], P(('path', 'tensor')), may hold values from -120 to 120
- teacher: bfloat16 [12288, 2048], P('path'), may hold values from -3 to 3
- params: bfloat16 [3, 3, 7168, 2048], P(None, None, ('tensor', 'path')), may hold values from -4 to 4
- momentum: float32 [3, 3, 7168, 2048], P(None, None, ('tensor', 'path')), may hold values from -3 to 3
- path_alive: int32 [32], replicated, may hold values from 0 to 1, as said below
- path_module: int32 [32], replicated, may hold values from 0 to 2, as said below
Outputs:
- new_params: bfloat16 [3, 3, 7168, 2048], P(None, None, ('tensor', 'path'))
- new_momentum: float32 [3, 3, 7168, 2048], P(None, None, ('tensor', 'path'))
Inputs may be any that keep to these rules, and one draw needn't show every extreme that they name: `path_alive`: at least one path is dead. `path_module`: every one of the 3 modules is used by at least one path whose path_alive entry is 1.
All inputs are finite; a program needn't handle non-finite values.
Results may differ from a plain program's by a relative error of at most 0.0047.
Values may be sent and summed in bfloat16 or wider, within the bound.
No kernel may reach another device: no remote copies, remote signals or barrier semaphores. Data moves between devices by JAX's collectives and lax.ppermute only.
A program may use at most 64 MiB of HBM per device.

v0:
```python
import math
import jax
import jax.numpy as jnp
from jax import lax
from jax.sharding import PartitionSpec as P

D = 2048
FW = 7168


def per_device(hidden_in, teacher, params, momentum, path_alive, path_module):
    module_count = params.shape[0]
    block_rows = params.shape[2]
    width = params.shape[3]
    path_count = path_alive.shape[0]
    contract_last = (((1,), (1,)), ((), ()))
    contract_first = (((0,), (0,)), ((), ()))
    picked = jnp.transpose(jnp.take(params, path_module, axis=0, mode="clip"), (1, 2, 0, 3))
    rows = lax.all_to_all(picked, "path", split_axis=2, concat_axis=2, tiled=True)
    local_rows = path_count * block_rows
    rows = rows.reshape(3, local_rows, width)
    gate_rows, up_rows, down_rows = (rows[0], rows[1], rows[2])
    own = hidden_in.astype(jnp.float32)
    mean_sq = jnp.mean(jnp.square(own), axis=1, keepdims=True)
    own_normed = (own * lax.rsqrt(mean_sq + 1e-05)).astype(jnp.bfloat16)
    normed = lax.all_gather(own_normed, "tensor", axis=0, tiled=True)
    gate_pre = lax.dot_general(
        normed, gate_rows, contract_last, preferred_element_type=jnp.float32
    ) / math.sqrt(D)
    up_proj = lax.dot_general(
        normed, up_rows, contract_last, preferred_element_type=jnp.float32
    ) / math.sqrt(D)
    sigmoid_gate = jax.nn.sigmoid(gate_pre)
    activated = gate_pre * sigmoid_gate
    hidden = (activated * up_proj).astype(jnp.bfloat16)
    partial_out = jnp.dot(hidden, down_rows, preferred_element_type=jnp.float32) / math.sqrt(FW)
    output = lax.psum(partial_out, "tensor")
    cotangent = (4.0 * (output - teacher.astype(jnp.float32))).astype(jnp.bfloat16)
    piece_shape = (block_rows, path_count, width)

    def send_back(delta):
        return lax.all_to_all(
            delta.reshape(piece_shape), "path", split_axis=1, concat_axis=1, tiled=True
        )

    down_delta = (
        lax.dot_general(hidden, cotangent, contract_first, preferred_element_type=jnp.float32)
        / math.sqrt(FW)
    ).astype(jnp.bfloat16)
    down_got = send_back(down_delta)
    hidden_grad = lax.dot_general(
        cotangent, down_rows, contract_last, preferred_element_type=jnp.float32
    ) / math.sqrt(FW)
    gate_grad = (
        hidden_grad * up_proj * sigmoid_gate * (1.0 + gate_pre * (1.0 - sigmoid_gate))
    ).astype(jnp.bfloat16)
    up_grad = (hidden_grad * activated).astype(jnp.bfloat16)
    gate_delta = (
        lax.dot_general(gate_grad, normed, contract_first, preferred_element_type=jnp.float32)
        / math.sqrt(D)
    ).astype(jnp.bfloat16)
    gate_got = send_back(gate_delta)
    up_delta = (
        lax.dot_general(up_grad, normed, contract_first, preferred_element_type=jnp.float32)
        / math.sqrt(D)
    ).astype(jnp.bfloat16)
    up_got = send_back(up_delta)
    member = (path_module[:, None] == jnp.arange(module_count, dtype=jnp.int32)[None, :]).astype(
        jnp.int32
    ) * path_alive[:, None]
    counts = jnp.sum(member, axis=0).astype(jnp.float32)
    new_momentum = []
    new_params = []
    weighting = member.astype(jnp.bfloat16)
    for j, got in enumerate((gate_got, up_got, down_got)):
        got, weighting_j, momentum_j, params_j = lax.optimization_barrier(
            (got, weighting, momentum[:, j], params[:, j])
        )
        summed = lax.dot_general(
            weighting_j, got, (((0,), (1,)), ((), ())), preferred_element_type=jnp.float32
        )
        mean_delta = summed / counts[:, None, None]
        momentum_j = 0.9 * momentum_j + mean_delta
        params_j = (params_j.astype(jnp.float32) - 0.7 * (mean_delta + 0.9 * momentum_j)).astype(
            jnp.bfloat16
        )
        new_momentum.append(momentum_j)
        new_params.append(params_j)
    new_momentum = jnp.stack(new_momentum, axis=1)
    new_params = jnp.stack(new_params, axis=1)
    return (new_params, new_momentum)


def solution(mesh):
    return jax.shard_map(
        per_device,
        mesh=mesh,
        in_specs=(
            P(("path", "tensor"), None),
            P("path", None),
            P(None, None, ("tensor", "path"), None),
            P(None, None, ("tensor", "path"), None),
            P(),
            P(),
        ),
        out_specs=(
            P(None, None, ("tensor", "path"), None),
            P(None, None, ("tensor", "path"), None),
        ),
        check_vma=False,
    )
```

profile of v0, /device:TPU:1, one launch (start us, length us, event | category | flops | bytes accessed | tf_op | source)
XLA Modules:
  0.0 409.1 jit_solution(1168579440316608955)
XLA Ops:
  7.2 0.7 pad_clamp_fusion
  7.8 4.6 %gather_fusion = bf16[32,3,14,2048]{3,2,1,0:T(8,128)(2,1)} fusion(bf16[3,3,14,2048]{3,2,1,0:T(8,128)(2,1)} %param.8, s32[1024]{0:T(1024)S(1)} %pad_clamp_fusion), kind=kCustom, calls=%fused_computation | custom fusion | bytes 11010176 | tf_op jit(solution)/shard_map/jit(_take)/gather | solution.py:18
  12.5 11.5 %all-to-all-start = ((bf16[3,14,32,2048]{3,1,0,2:T(8,128)(2,1)}), bf16[3,14,32,2048]{3,1,0,2:T(8,128)(2,1)}, u32[]{:S(2)}, u32[]{:S(2)}) async-start(bf16[3,14,32,2048]{3,1,0,2:T(8,128)(2,1)} %bitcast.60), calls=%async_computation | async-start | bytes 12582912 | tf_op jit(solution)/shard_map/all_to_all | solution.py:19
  23.9 0.0 all-gather.2.cloned.1.call-start
  24.0 0.1 fusion.11
  24.1 0.7 fusion.12
  24.9 0.0 all-gather.2.cloned.1.call-update
  24.9 0.0 all-reduce.2.cloned.1.call-start
  24.9 76.3 %all-to-all-done = bf16[3,14,32,2048]{3,1,0,2:T(8,128)(2,1)} async-done(((bf16[3,14,32,2048]{3,1,0,2:T(8,128)(2,1)}), bf16[3,14,32,2048]{3,1,0,2:T(8,128)(2,1)}, u32[]{:S(2)}, u32[]{:S(2)}) %all-to-all-start) | async-done | bytes 5505056 | tf_op jit(solution)/shard_map/all_to_all | solution.py:19
  101.3 4.0 fusion.19
  105.3 2.2 copy.35
  107.5 2.3 copy.36
  109.8 1.0 copy.37
  110.8 0.0 all-gather.2.cloned.1.call-done
  110.8 3.3 convolution_multiply_fusion.3
  114.1 2.0 multiply_convert_fusion.6
  116.1 0.7 copy-done.3
  116.8 2.7 convolution_multiply_fusion
  119.6 149.8 %all-reduce.2.cloned.1.call-done = f32[384,2048]{1,0:T(8,128)} async-done(((f32[384,2048]{1,0:T(8,128)}), f32[384,2048]{1,0:T(8,128)}) %all-reduce.2.cloned.1.call-update) | async-done | bytes 3145744 | tf_op jit(solution)/shard_map/psum | solution.py:37
  269.4 3.2 convolution_multiply_fusion.1
  272.6 1.1 multiply_convert_fusion.1
  273.8 2.3 copy.42
  276.2 17.1 %all-to-all-start.2 = ((bf16[14,32,2048]{2,0,1:T(8,128)(2,1)}), bf16[14,32,2048]{2,0,1:T(8,128)(2,1)}, u32[]{:S(2)}, u32[]{:S(2)}) async-start(bf16[14,32,2048]{2,0,1:T(8,128)(2,1)} %copy.42), calls=%async_computation.2 | async-start | bytes 4194304 | tf_op jit(solution)/shard_map/all_to_all | solution.py:42
  293.3 2.4 multiply_convert_fusion.2
  295.6 2.4 copy.38
  298.1 23.6 %all-to-all-done.2 = bf16[14,32,2048]{2,0,1:T(8,128)(2,1)} async-done(((bf16[14,32,2048]{2,0,1:T(8,128)(2,1)}), bf16[14,32,2048]{2,0,1:T(8,128)(2,1)}, u32[]{:S(2)}, u32[]{:S(2)}) %all-to-all-start.2) | async-done | bytes 1835040 | tf_op jit(solution)/shard_map/all_to_all | solution.py:42
  321.6 5.2 %all-to-all-start.1 = ((bf16[14,32,2048]{2,0,1:T(8,128)(2,1)}), bf16[14,32,2048]{2,0,1:T(8,128)(2,1)}, u32[]{:S(2)}, u32[]{:S(2)}) async-start(bf16[14,32,2048]{2,0,1:T(8,128)(2,1)} %copy.38), calls=%async_computation.1 | async-start | bytes 4194304 | tf_op jit(solution)/shard_map/all_to_all | solution.py:42
  326.8 2.6 multiply_convert_fusion
  329.4 2.4 copy.46
  331.7 23.5 %all-to-all-done.1 = bf16[14,32,2048]{2,0,1:T(8,128)(2,1)} async-done(((bf16[14,32,2048]{2,0,1:T(8,128)(2,1)}), bf16[14,32,2048]{2,0,1:T(8,128)(2,1)}, u32[]{:S(2)}, u32[]{:S(2)}) %all-to-all-start.1) | async-done | bytes 1835040 | tf_op jit(solution)/shard_map/all_to_all | solution.py:42
  355.3 4.5 %all-to-all-start.3 = ((bf16[14,32,2048]{2,0,1:T(8,128)(2,1)}), bf16[14,32,2048]{2,0,1:T(8,128)(2,1)S(1)}, u32[]{:S(2)}, u32[]{:S(2)}) async-start(bf16[14,32,2048]{2,0,1:T(8,128)(2,1)} %copy.46), calls=%async_computation.3 | async-start | bytes 4194304 | tf_op jit(solution)/shard_map/all_to_all | solution.py:42
  359.8 0.1 fusion.20
  359.9 0.2 copy.75
  360.1 0.7 copy-done
  360.9 0.8 copy.78
  361.7 0.1 select_reduce_fusion
  361.8 0.2 copy.76
  362.1 0.8 copy.79
  362.9 0.2 copy.74
  363.2 0.8 copy.77
  364.0 24.2 %all-to-all-done.3 = bf16[14,32,2048]{2,0,1:T(8,128)(2,1)S(1)} async-done(((bf16[14,32,2048]{2,0,1:T(8,128)(2,1)}), bf16[14,32,2048]{2,0,1:T(8,128)(2,1)S(1)}, u32[]{:S(2)}, u32[]{:S(2)}) %all-to-all-start.3) | async-done | bytes 1835040 | tf_op jit(solution)/shard_map/all_to_all | solution.py:42
  388.2 3.7 convolution_divide_fusion.1
  391.9 2.2 fusion.6
  394.1 4.1 %fusion.4 = (f32[3,1,14,2048]{3,0,2,1:T(4,128)S(1)}, bf16[3,1,14,2048]{3,0,2,1:T(4,128)(2,1)S(1)}, bf16[3,1,14,2048]{3,0,2,1:T(4,128)(2,1)S(1)}, f32[3,1,14,2048]{3,0,2,1:T(4,128)S(1)}) fusion(f32[3,14,2048]{2,0,1:T(4,128)S(1)} %bitcast.69, bf16[3,14,2048]{2,0,1:T(4,128)(2,1)S(1)} %bitcast.72, f32[3,14,2048]{2,0,1:T(4,128)S(1)} %convolution_divide_fusion.1, ...), kind=kOutput, calls=%fused_computation.31 | convolution fusion | flops 6967296 | bytes 4243660 | tf_op jit(solution)/shard_map/dot_general | solution.py:79
  398.3 0.6 pad_maximum_fusion
  398.9 1.6 copy.51
  400.5 0.6 pad_maximum_fusion.1
  401.1 1.2 copy.50
  (44 shorter events, 0.2 us)
Async XLA Ops:
  12.5 11.5 %copy-start.9 = (bf16[24,2048]{1,0:T(8,128)(2,1)S(1)}, bf16[24,2048]{1,0:T(8,128)(2,1)}, u32[]{:S(2)}) copy-start(bf16[24,2048]{1,0:T(8,128)(2,1)} %param.6) | copy-start | bytes 294916
  12.5 88.8 %all-to-all-start = ((bf16[3,14,32,2048]{3,1,0,2:T(8,128)(2,1)}), bf16[3,14,32,2048]{3,1,0,2:T(8,128)(2,1)}, u32[]{:S(2)}, u32[]{:S(2)}) async-start(bf16[3,14,32,2048]{3,1,0,2:T(8,128)(2,1)} %bitcast.60), calls=%async_computation | async-start | bytes 12582912 | tf_op jit(solution)/shard_map/all_to_all | solution.py:19
  23.9 86.9 %all-gather.2.cloned.1.call-start = ((), (), s32[]{:S(2)}) async-start(), calls=%async_computation.4 | async-start | bytes 1671168 | tf_op jit(solution)/shard_map/all_gather | solution.py:26
  24.9 244.5 %all-reduce.2.cloned.1.call-start = ((), (), s32[]{:S(2)}) async-start(), calls=%async_computation.5 | async-start | bytes 6291456 | tf_op jit(solution)/shard_map/psum | solution.py:37
  110.8 3.3 copy-start.5
  110.8 3.3 copy-start.15
  114.1 2.0 copy-start.18
  116.1 0.7 copy-start.3
  119.6 149.9 %copy-start.2 = (bf16[384,2048]{1,0:T(8,128)(2,1)S(1)}, bf16[384,2048]{1,0:T(8,128)(2,1)}, u32[]{:S(2)}) copy-start(bf16[384,2048]{1,0:T(8,128)(2,1)} %param.7) | copy-start | bytes 4718596
  269.4 3.2 copy-start.16
  269.4 3.2 copy-start.19
  272.6 1.2 copy-start.7
  276.1 17.1 %copy-start.8 = (f32[384,448]{0,1:T(8,128)S(1)}, f32[384,448]{0,1:T(8,128)}, u32[]{:S(2)}) copy-start(f32[384,448]{0,1:T(8,128)} %copy-done.7) | copy-start | bytes 2064388
  276.1 17.1 %copy-start.17 = (bf16[384,2048]{1,0:T(8,128)(2,1)S(1)}, bf16[384,2048]{1,0:T(8,128)(2,1)}, u32[]{:S(2)}) copy-start(bf16[384,2048]{1,0:T(8,128)(2,1)} %all-gather.2.cloned.1.call-done) | copy-start | bytes 4718596
  276.2 17.1 %copy-start.20 = (f32[384,448]{0,1:T(8,128)S(1)}, f32[384,448]{0,1:T(8,128)}, u32[]{:S(2)}) copy-start(f32[384,448]{0,1:T(8,128)} %copy-done.18) | copy-start | bytes 2064388
  276.2 45.5 %all-to-all-start.2 = ((bf16[14,32,2048]{2,0,1:T(8,128)(2,1)}), bf16[14,32,2048]{2,0,1:T(8,128)(2,1)}, u32[]{:S(2)}, u32[]{:S(2)}) async-start(bf16[14,32,2048]{2,0,1:T(8,128)(2,1)} %copy.42), calls=%async_computation.2 | async-start | bytes 4194304 | tf_op jit(solution)/shard_map/all_to_all | solution.py:42
  298.0 28.7 %copy-start.1 = (f32[384,2048]{1,0:T(8,128)S(1)}, f32[384,2048]{1,0:T(8,128)}, u32[]{:S(2)}) copy-start(f32[384,2048]{1,0:T(8,128)} %all-reduce.2.cloned.1.call-done) | copy-start | bytes 9437188
  298.0 28.7 %copy-start.4 = (bf16[384,448]{0,1:T(8,128)(2,1)S(1)}, bf16[384,448]{0,1:T(8,128)(2,1)}, u32[]{:S(2)}) copy-start(bf16[384,448]{0,1:T(8,128)(2,1)} %copy-done.3) | copy-start | bytes 1032196
  321.6 33.6 %all-to-all-start.1 = ((bf16[14,32,2048]{2,0,1:T(8,128)(2,1)}), bf16[14,32,2048]{2,0,1:T(8,128)(2,1)}, u32[]{:S(2)}, u32[]{:S(2)}) async-start(bf16[14,32,2048]{2,0,1:T(8,128)(2,1)} %copy.38), calls=%async_computation.1 | async-start | bytes 4194304 | tf_op jit(solution)/shard_map/all_to_all | solution.py:42
  331.7 28.0 %copy-start.6 = (f32[3,3,14,2048]{3,2,1,0:T(8,128)S(1)}, f32[3,3,14,2048]{3,2,1,0:T(8,128)}, u32[]{:S(2)}) copy-start(f32[3,3,14,2048]{3,2,1,0:T(8,128)} %param.9) | copy-start | bytes 3096580
  355.3 32.9 %all-to-all-start.3 = ((bf16[14,32,2048]{2,0,1:T(8,128)(2,1)}), bf16[14,32,2048]{2,0,1:T(8,128)(2,1)S(1)}, u32[]{:S(2)}, u32[]{:S(2)}) async-start(bf16[14,32,2048]{2,0,1:T(8,128)(2,1)} %copy.46), calls=%async_computation.3 | async-start | bytes 4194304 | tf_op jit(solution)/shard_map/all_to_all | solution.py:42
  359.8 1.1 copy-start
  359.8 1.9 copy-start.13
  359.8 1.9 copy-start.14
  388.2 3.7 copy-start.12
  391.9 2.3 copy-start.10
  391.9 2.3 copy-start.11
Sparse Core Ops, SparseCore 0:
  27.4 64.8 all-gather.1
  119.7 149.6 all-reduce.1
where the time goes:
time: 410 us; the launch traced here: 409 us
  waiting for transfers between devices  297 us (72%)
  starting transfers between devices  38.2 us (9%)
  local copies, waits for them, and re-layouts  29 us (7%)
  matrix products  27.3 us (7%)
  between operations  14.4 us (4%)
    psum x1, waiting for transfers between devices, per_device(): output = lax.psum(partial_out, 'tensor')  150 us
    all_to_all x1, waiting for transfers between devices, per_device(): lax.all_to_all(picked, 'path', split_axis=2, concat_axis=2, tiled=True)  76.3 us
    all_to_all x3, waiting for transfers between devices, send_back(): lax.all_to_all(delta.reshape(piece_shape), 'path', split_axis=1, concat_a...  71.2 us
    all_to_all x3, starting transfers between devices, send_back(): lax.all_to_all(delta.reshape(piece_shape), 'path', split_axis=1, concat_a...  26.7 us
    all_to_all x1, starting transfers between devices, per_device(): lax.all_to_all(picked, 'path', split_axis=2, concat_axis=2, tiled=True)  11.5 us
    dot_general x3, matrix products, per_device(): lax.dot_general(weighting_j, got, (((0,), (1,)), ((), ())), preferred_ele...  10.1 us
    slice x4, local copies, waits for them, and re-layouts, per_device(): gate_rows, up_rows, down_rows = (rows[0], rows[1], rows[2])  9.49 us
  transfers between devices with their start and end apart: 6, of which 5 were waited for; matrix products, arithmetic and copies ran while one was open for 6% of the time, Pallas kernels for 0%

commit v1 on v0

--- a/solution.py
+++ b/solution.py
@@ -1,11 +1,31 @@
+import functools
 import math
 import jax
 import jax.numpy as jnp
 from jax import lax
 from jax.sharding import PartitionSpec as P
+from jax.lax import axis_size, ppermute
 
 D = 2048
 FW = 7168
+
+
+def entries_reach(chunk, peer_axis):
+    world = axis_size(peer_axis)
+
+    def bring_results(new, wide_out):
+        if wide_out >= world:
+            return new
+        t_next = tuple(((k0, k0 ^ wide_out) for k0 in range(world)))
+        current_value = ppermute(new, axis_name=peer_axis, perm=t_next)
+        taken_in = bring_results(new + current_value, 2 * wide_out)
+        return taken_in
+
+    tile_out = bring_results(chunk, 1)
+    return tile_out
+
+
+keep_up_field_up = functools.partial(entries_reach, peer_axis="tensor")
 
 
 def per_device(hidden_in, teacher, params, momentum, path_alive, path_module):
@@ -34,7 +54,7 @@
     activated = gate_pre * sigmoid_gate
     hidden = (activated * up_proj).astype(jnp.bfloat16)
     partial_out = jnp.dot(hidden, down_rows, preferred_element_type=jnp.float32) / math.sqrt(FW)
-    output = lax.psum(partial_out, "tensor")
+    output = keep_up_field_up(partial_out)
     cotangent = (4.0 * (output - teacher.astype(jnp.float32))).astype(jnp.bfloat16)
     piece_shape = (block_rows, path_count, width)
 

time: 410 us -> 1100 us (2.68)
  waiting for transfers between devices: 297 us -> 821 us
  starting transfers between devices: 38.2 us -> 201 us
    ppermute x0 -> x4, waiting for transfers between devices: none -> 674 us  [bring_results(): current_value = ppermute(new, axis_name=peer_axis, perm=t_next)]
    psum x1 -> x0, waiting for transfers between devices: 150 us -> none  [per_device(): output = lax.psum(partial_out, 'tensor')]
    all_to_all x3, starting transfers between devices: 26.7 us -> 169 us  [send_back(): lax.all_to_all(delta.reshape(piece_shape), 'path', split_axis=1, concat_a...]
    ppermute x0 -> x4, starting transfers between devices: none -> 20.6 us  [bring_results(): current_value = ppermute(new, axis_name=peer_axis, perm=t_next)]
  transfers between devices with their start and end apart: 6 -> 9, of which waited for: 5 -> 8; matrix products, arithmetic and copies ran while one was open for 6% -> 2% of each run, Pallas kernels for 0% -> 0%
where the time goes in v1:
time: 1100 us; the launch traced here: 1090 us
  waiting for transfers between devices  821 us (75%)
  starting transfers between devices  201 us (18%)
  local copies, waits for them, and re-layouts  28.1 us (3%)
  matrix products  24.2 us (2%)
  between operations  14.4 us (1%)
    ppermute x4, waiting for transfers between devices, bring_results(): current_value = ppermute(new, axis_name=peer_axis, perm=t_next)  674 us
    all_to_all x3, starting transfers between devices, send_back(): lax.all_to_all(delta.reshape(piece_shape), 'path', split_axis=1, concat_a...  169 us
    all_to_all x1, waiting for transfers between devices, per_device(): lax.all_to_all(picked, 'path', split_axis=2, concat_axis=2, tiled=True)  76.4 us
    all_to_all x3, waiting for transfers between devices, send_back(): lax.all_to_all(delta.reshape(piece_shape), 'path', split_axis=1, concat_a...  70.7 us
  transfers between devices with their start and end apart: 9, of which 8 were waited for; matrix products, arithmetic and copies ran while one was open for 2% of the time, Pallas kernels for 0%

profile of v1, /device:TPU:1, one launch (start us, length us, event | category | flops | bytes accessed | tf_op | source)
XLA Modules:
  0.0 1094.4 jit_solution(1403604534323607856)
XLA Ops:
  7.2 0.7 pad_clamp_fusion
  7.8 4.6 gather_fusion
  12.4 11.5 %all-to-all-start = ((bf16[3,14,32,2048]{3,1,0,2:T(8,128)(2,1)}), bf16[3,14,32,2048]{3,1,0,2:T(8,128)(2,1)}, u32[]{:S(2)}, u32[]{:S(2)}) async-start(bf16[3,14,32,2048]{3,1,0,2:T(8,128)(2,1)} %bitcast.62), calls=%async_computation | async-start | bytes 12582912 | tf_op jit(solution)/shard_map/all_to_all | solution.py:39
  24.1 0.7 fusion.12
  24.9 76.4 %all-to-all-done = bf16[3,14,32,2048]{3,1,0,2:T(8,128)(2,1)} async-done(((bf16[3,14,32,2048]{3,1,0,2:T(8,128)(2,1)}), bf16[3,14,32,2048]{3,1,0,2:T(8,128)(2,1)}, u32[]{:S(2)}, u32[]{:S(2)}) %all-to-all-start) | async-done | bytes 5505056 | tf_op jit(solution)/shard_map/all_to_all | solution.py:39
  101.3 4.0 fusion.19
  105.3 2.3 copy.35
  107.5 2.2 copy.36
  109.7 1.0 copy.37
  110.8 3.3 convolution_multiply_fusion.3
  114.1 2.0 multiply_convert_fusion.6
  116.1 1.0 convolution_multiply_fusion
  117.1 1.9 collective-permute-start
  119.0 66.7 %collective-permute-done = f32[384,2048]{1,0:T(8,128)S(1)} collective-permute-done((f32[384,2048]{1,0:T(8,128)S(1)}, f32[384,2048]{1,0:T(8,128)S(1)}, u32[]{:S(2)}, u32[]{:S(2)}) %collective-permute-start) | collective-permute-done | bytes 3145760 | tf_op jit(solution)/shard_map/ppermute | solution.py:20
  185.7 0.7 add.46
  186.4 1.9 collective-permute-start.1
  188.3 138.3 %collective-permute-done.1 = f32[384,2048]{1,0:T(8,128)S(1)} collective-permute-done((f32[384,2048]{1,0:T(8,128)S(1)}, f32[384,2048]{1,0:T(8,128)S(1)}, u32[]{:S(2)}, u32[]{:S(2)}) %collective-permute-start.1) | collective-permute-done | bytes 3145760 | tf_op jit(solution)/shard_map/ppermute | solution.py:20
  326.6 0.6 add.47
  327.2 5.5 collective-permute-start.2
  332.7 339.7 %collective-permute-done.2 = f32[384,2048]{1,0:T(8,128)S(1)} collective-permute-done((f32[384,2048]{1,0:T(8,128)S(1)}, f32[384,2048]{1,0:T(8,128)S(1)}, u32[]{:S(2)}, u32[]{:S(2)}) %collective-permute-start.2) | collective-permute-done | bytes 3145760 | tf_op jit(solution)/shard_map/ppermute | solution.py:20
  672.4 0.6 add.48
  673.0 11.3 %collective-permute-start.3 = (f32[384,2048]{1,0:T(8,128)S(1)}, f32[384,2048]{1,0:T(8,128)S(1)}, u32[]{:S(2)}, u32[]{:S(2)}) collective-permute-start(f32[384,2048]{1,0:T(8,128)S(1)} %add.48), channel_id=1, source_target_pairs={{0,8},{1,9},{2,10},{3,11},{4,12},{5,13},{6,14},{7,15},{8,0},{9,1},... | collective-permute-start | bytes 9437192 | tf_op jit(solution)/shard_map/ppermute | solution.py:20
  684.2 129.2 %collective-permute-done.3 = f32[384,2048]{1,0:T(8,128)S(1)} collective-permute-done((f32[384,2048]{1,0:T(8,128)S(1)}, f32[384,2048]{1,0:T(8,128)S(1)}, u32[]{:S(2)}, u32[]{:S(2)}) %collective-permute-start.3) | collective-permute-done | bytes 3145760 | tf_op jit(solution)/shard_map/ppermute | solution.py:20
  813.4 0.9 multiply_convert_fusion.3
  814.3 1.1 convolution_multiply_fusion.1
  815.5 1.1 multiply_convert_fusion.1
  816.7 2.4 copy.42
  819.0 158.8 %all-to-all-start.2 = ((bf16[14,32,2048]{2,0,1:T(8,128)(2,1)}), bf16[14,32,2048]{2,0,1:T(8,128)(2,1)S(1)}, u32[]{:S(2)}, u32[]{:S(2)}) async-start(bf16[14,32,2048]{2,0,1:T(8,128)(2,1)} %copy.42), calls=%async_computation.2 | async-start | bytes 4194304 | tf_op jit(solution)/shard_map/all_to_all | solution.py:62
  977.8 3.1 multiply_convert_fusion.2
  980.9 2.3 copy.38
  983.2 22.9 %all-to-all-done.2 = bf16[14,32,2048]{2,0,1:T(8,128)(2,1)S(1)} async-done(((bf16[14,32,2048]{2,0,1:T(8,128)(2,1)}), bf16[14,32,2048]{2,0,1:T(8,128)(2,1)S(1)}, u32[]{:S(2)}, u32[]{:S(2)}) %all-to-all-start.2) | async-done | bytes 1835040 | tf_op jit(solution)/shard_map/all_to_all | solution.py:62
  1006.2 5.2 all-to-all-start.1
  1011.3 2.5 multiply_convert_fusion
  1013.9 2.4 copy.46
  1016.2 23.6 %all-to-all-done.1 = bf16[14,32,2048]{2,0,1:T(8,128)(2,1)} async-done(((bf16[14,32,2048]{2,0,1:T(8,128)(2,1)}), bf16[14,32,2048]{2,0,1:T(8,128)(2,1)}, u32[]{:S(2)}, u32[]{:S(2)}) %all-to-all-start.1) | async-done | bytes 1835040 | tf_op jit(solution)/shard_map/all_to_all | solution.py:62
  1039.8 5.2 all-to-all-start.3
  1045.4 0.7 copy-done
  1046.1 0.8 copy.78
  1047.3 0.8 copy.79
  1048.4 0.8 copy.77
  1049.2 24.2 %all-to-all-done.3 = bf16[14,32,2048]{2,0,1:T(8,128)(2,1)} async-done(((bf16[14,32,2048]{2,0,1:T(8,128)(2,1)}), bf16[14,32,2048]{2,0,1:T(8,128)(2,1)}, u32[]{:S(2)}, u32[]{:S(2)}) %all-to-all-start.3) | async-done | bytes 1835040 | tf_op jit(solution)/shard_map/all_to_all | solution.py:62
  1073.5 2.1 convolution_divide_fusion.1
  1075.5 3.9 fusion.6
  1079.4 4.1 fusion.4
  1083.6 0.6 pad_maximum_fusion
  1084.2 1.6 copy.51
  1085.8 0.6 pad_maximum_fusion.1
  1086.4 1.2 copy.50
  (37 shorter events, 1.2 us)
Async XLA Ops:
  12.4 11.5 %copy-start.5 = (bf16[24,2048]{1,0:T(8,128)(2,1)S(1)}, bf16[24,2048]{1,0:T(8,128)(2,1)}, u32[]{:S(2)}) copy-start(bf16[24,2048]{1,0:T(8,128)(2,1)} %param.6) | copy-start | bytes 294916
  12.4 88.8 %all-to-all-start = ((bf16[3,14,32,2048]{3,1,0,2:T(8,128)(2,1)}), bf16[3,14,32,2048]{3,1,0,2:T(8,128)(2,1)}, u32[]{:S(2)}, u32[]{:S(2)}) async-start(bf16[3,14,32,2048]{3,1,0,2:T(8,128)(2,1)} %bitcast.62), calls=%async_computation | async-start | bytes 12582912 | tf_op jit(solution)/shard_map/all_to_all | solution.py:39
  23.9 86.9 %all-gather.2.cloned.1.call-start = ((), (), s32[]{:S(2)}) async-start(), calls=%async_computation.4 | async-start | bytes 1671168 | tf_op jit(solution)/shard_map/all_gather | solution.py:46
  110.8 3.3 copy-start.1
  110.8 3.3 copy-start.11
  117.1 68.6 %collective-permute-start = (f32[384,2048]{1,0:T(8,128)S(1)}, f32[384,2048]{1,0:T(8,128)S(1)}, u32[]{:S(2)}, u32[]{:S(2)}) collective-permute-start(f32[384,2048]{1,0:T(8,128)S(1)} %convolution_multiply_fusion), channel_id=1, source_target_pairs={{0,1},{1,0},{2,3},{3,2},{4,5},{5,4},{6,7},{7,6},{8,9},{9,8},{10,11... | collective-permute-start | bytes 9437192 | tf_op jit(solution)/shard_map/ppermute | solution.py:20
  186.4 140.2 %collective-permute-start.1 = (f32[384,2048]{1,0:T(8,128)S(1)}, f32[384,2048]{1,0:T(8,128)S(1)}, u32[]{:S(2)}, u32[]{:S(2)}) collective-permute-start(f32[384,2048]{1,0:T(8,128)S(1)} %add.46), channel_id=1, source_target_pairs={{0,2},{1,3},{2,0},{3,1},{4,6},{5,7},{6,4},{7,5},{8,10},{9,11},{10,... | collective-permute-start | bytes 9437192 | tf_op jit(solution)/shard_map/ppermute | solution.py:20
  327.2 486.3 %copy-start.2 = (bf16[384,2048]{1,0:T(8,128)(2,1)S(1)}, bf16[384,2048]{1,0:T(8,128)(2,1)}, u32[]{:S(2)}) copy-start(bf16[384,2048]{1,0:T(8,128)(2,1)} %param.7) | copy-start | bytes 4718596
  327.2 345.2 %collective-permute-start.2 = (f32[384,2048]{1,0:T(8,128)S(1)}, f32[384,2048]{1,0:T(8,128)S(1)}, u32[]{:S(2)}, u32[]{:S(2)}) collective-permute-start(f32[384,2048]{1,0:T(8,128)S(1)} %add.47), channel_id=1, source_target_pairs={{0,4},{1,5},{2,6},{3,7},{4,0},{5,1},{6,2},{7,3},{8,12},{9,13},{10,... | collective-permute-start | bytes 9437192 | tf_op jit(solution)/shard_map/ppermute | solution.py:20
  673.0 140.5 %collective-permute-start.3 = (f32[384,2048]{1,0:T(8,128)S(1)}, f32[384,2048]{1,0:T(8,128)S(1)}, u32[]{:S(2)}, u32[]{:S(2)}) collective-permute-start(f32[384,2048]{1,0:T(8,128)S(1)} %add.48), channel_id=1, source_target_pairs={{0,8},{1,9},{2,10},{3,11},{4,12},{5,13},{6,14},{7,15},{8,0},{9,1},... | collective-permute-start | bytes 9437192 | tf_op jit(solution)/shard_map/ppermute | solution.py:20
  814.3 1.2 copy-start.3
  815.5 1.2 copy-start.12
  819.0 187.1 %all-to-all-start.2 = ((bf16[14,32,2048]{2,0,1:T(8,128)(2,1)}), bf16[14,32,2048]{2,0,1:T(8,128)(2,1)S(1)}, u32[]{:S(2)}, u32[]{:S(2)}) async-start(bf16[14,32,2048]{2,0,1:T(8,128)(2,1)} %copy.42), calls=%async_computation.2 | async-start | bytes 4194304 | tf_op jit(solution)/shard_map/all_to_all | solution.py:62
  1006.2 33.6 %all-to-all-start.1 = ((bf16[14,32,2048]{2,0,1:T(8,128)(2,1)}), bf16[14,32,2048]{2,0,1:T(8,128)(2,1)}, u32[]{:S(2)}, u32[]{:S(2)}) async-start(bf16[14,32,2048]{2,0,1:T(8,128)(2,1)} %copy.38), calls=%async_computation.1 | async-start | bytes 4194304 | tf_op jit(solution)/shard_map/all_to_all | solution.py:62
  1016.2 28.8 %copy-start.4 = (f32[3,3,14,2048]{3,2,1,0:T(8,128)S(1)}, f32[3,3,14,2048]{3,2,1,0:T(8,128)}, u32[]{:S(2)}) copy-start(f32[3,3,14,2048]{3,2,1,0:T(8,128)} %param.9) | copy-start | bytes 3096580
  1039.8 33.7 %all-to-all-start.3 = ((bf16[14,32,2048]{2,0,1:T(8,128)(2,1)}), bf16[14,32,2048]{2,0,1:T(8,128)(2,1)}, u32[]{:S(2)}, u32[]{:S(2)}) async-start(bf16[14,32,2048]{2,0,1:T(8,128)(2,1)} %copy.46), calls=%async_computation.3 | async-start | bytes 4194304 | tf_op jit(solution)/shard_map/all_to_all | solution.py:62
  1045.0 1.1 copy-start
  1045.0 1.9 copy-start.9
  1045.0 1.9 copy-start.10
  1073.5 2.1 copy-start.8
  1075.5 3.9 copy-start.6
  1075.5 3.9 copy-start.7
Sparse Core Ops, SparseCore 0:
  27.4 64.7 all-gather.1
